TPU v7x, 32 devices: a whole 2x2x4 slice. The times are simulated.
32 devices in a mesh: rep: 2 (over x), member: 4 (over y, core), tp: 4 (over z).
Axes of the slice: x: 2, y: 2, z: 4, core: 2. Of those that a mesh axis runs over, the one named last changes fastest.
Arguments:
- states: bfloat16 [4096, 1024], P(('rep', 'member', 'tp')), parts along dimension 0, may hold values from -6 to 6
- member_of: int32 [4096, 1], P(('rep', 'member', 'tp')), parts along dimension 0, may hold values from 0 to 1; in each aligned block of 128 rows (0 to 127, 128 to 255, ...) at most 128 rows name the same one
- place: int32 [4096], P(('rep', 'member', 'tp')), parts along dimension 0, may hold values from 0 to 2047, as said below
- norm_gain: float32 [2, 1024], replicated, may hold values from 0.5 to 2
- w_up: bfloat16 [4, 1024, 2048], P('member', None, 'tp'), may hold values from -0.1875 to 0.1875
- w_down: bfloat16 [4, 2048, 1024], P('member', 'tp'), may hold values from -0.09375 to 0.09375
- policy_gain: float32 [1024], replicated, may hold values from 0.5 to 2
- w_policy: bfloat16 [1024, 128], replicated, may hold values from -0.1875 to 0.1875
Outputs:
- imagined: bfloat16 [4096, 1024], P(('rep', 'member', 'tp')), parts along dimension 0
- action: bfloat16 [4096, 128], P(('rep', 'member', 'tp')), parts along dimension 0
There are 2 independent parts, one for each index of `rep`. A program takes and returns all parts, laid end to end along the dimension named above; an argument that names none is the same for every part. Nothing has to cross between parts.
Inputs may be any that keep to these rules, and one draw needn't show every extreme that they name: `member_of`: at most 128 of the rows of one device name any one member, and that count is reached on some device. `place`: A permutation of the 2048 learner positions; learner device k holds positions k * 128 to (k + 1) * 128 - 1, and the rows of each device go exactly 8 to every learner device.
All inputs are finite; a program needn't handle non-finite values.
Results may differ from a plain program's by a relative error of at most 0.0069.
Values may be sent and summed in bfloat16 or wider, within the bound.
No kernel may reach another device: no remote copies, remote signals or barrier semaphores. Data moves between devices by JAX's collectives and lax.ppermute only.
A program may use at most 128 MiB of HBM per device.

v0:
```python
import jax
import jax.numpy as jnp
from jax import lax
from jax.sharding import PartitionSpec as P

PARTIAL_DTYPE = jnp.bfloat16


def from_partner(value, axis, distance):
    return lax.ppermute(value, axis, [(i, i ^ 1 << distance) for i in range(lax.axis_size(axis))])


def from_chip_behind(value, axis, chips_back):
    size = lax.axis_size(axis)
    return lax.ppermute(value, axis, [(i, (i + 2 * chips_back) % size) for i in range(size)])


def swap_parts(value):
    n_rep = lax.axis_size("rep")
    return [value] + [
        lax.ppermute(value, "rep", [(i, (i + step) % n_rep) for i in range(n_rep)])
        for step in range(1, n_rep)
    ]


def fetch_shared(up, down, chips_back):
    n_rep = lax.axis_size("rep")
    share = up.shape[1] // n_rep
    rep_here = lax.axis_index("rep")
    got_up = from_chip_behind(
        lax.dynamic_slice_in_dim(up, rep_here * share, share, axis=1), "member", chips_back
    )
    got_up, down = lax.optimization_barrier((got_up, down))
    got_down = from_chip_behind(
        lax.dynamic_slice_in_dim(down, rep_here * share, share, axis=0), "member", chips_back
    )
    up_parts = swap_parts(got_up)
    down_parts = swap_parts(got_down)
    partner_up = [from_partner(part, "member", 0) for part in up_parts]
    partner_down = [from_partner(part, "member", 0) for part in down_parts]
    return (up_parts + partner_up, down_parts + partner_down)


def rms_scale(values, gain):
    mean_square = jnp.mean(values * values, axis=-1, keepdims=True)
    return values * lax.rsqrt(mean_square + 1e-06) * gain


def running_rank(member_hits):
    return jnp.sum((jnp.cumsum(member_hits, axis=0) - member_hits) * member_hits, axis=1)


def local(states, member_of, place, norm_gain, w_up, w_down, policy_gain, w_policy):
    n_member = lax.axis_size("member")
    n_tp = lax.axis_size("tp")
    n_dev = n_member * n_tp
    member_total = n_member // 2
    rows_here = states.shape[0]
    feature_width = states.shape[1]
    own_member = lax.axis_index("member") // 2
    own_block = (own_member, w_up[0], w_down[0])
    fetched = [
        ((own_member - back + member_total) % member_total, *fetch_shared(w_up[0], w_down[0], back))
        for back in range(1, member_total)
    ]
    per_learner = rows_here // n_dev
    learner = place // rows_here
    learner_hits = (learner[:, None] == jnp.arange(n_dev, dtype=jnp.int32)[None, :]).astype(
        jnp.int32
    )
    lane_index = learner * per_learner + running_rank(learner_hits)
    placer = jnp.arange(rows_here, dtype=jnp.int32)[:, None] == lane_index[None, :]
    states = jnp.dot(
        placer.astype(jnp.bfloat16), states, preferred_element_type=jnp.float32
    ).astype(jnp.bfloat16)
    member = jnp.sum(placer.astype(jnp.int32) * member_of[:, 0][None, :], axis=1)
    packed_spot = jnp.sum(placer.astype(jnp.int32) * (place % rows_here)[None, :], axis=1)
    gain_rows = jnp.take(norm_gain, member, axis=0)
    normed = rms_scale(states.astype(jnp.float32), gain_rows).astype(jnp.bfloat16)
    member_lanes = jnp.where(
        jnp.arange(128, dtype=jnp.int32)[None, :] == 0, member[:, None], 0
    ).astype(jnp.bfloat16)
    gathered = lax.all_gather(
        jnp.concatenate([normed, member_lanes], axis=1), "tp", axis=0, tiled=True
    )
    gathered_rows = gathered[:, :feature_width]
    gathered_member = gathered[:, feature_width].astype(jnp.int32)

    def apply_block(block_member, up_here, down_here):
        keep = (gathered_member == block_member).astype(jnp.bfloat16)[:, None]
        hidden = (
            jax.nn.gelu(jnp.dot(gathered_rows, up_here, preferred_element_type=jnp.float32)).astype(
                jnp.bfloat16
            )
            * keep
        )
        return jnp.dot(hidden, down_here, preferred_element_type=jnp.float32)

    def apply_pair(block_member, up_here, down_here):
        both_up = jnp.concatenate([up_here, from_partner(up_here, "member", 0)], axis=1)
        both_down = jnp.concatenate([down_here, from_partner(down_here, "member", 0)], axis=0)
        return apply_block(block_member, both_up, both_down)

    terms = [apply_pair(*own_block)]
    for block_member, up_here, down_here in fetched:
        terms, up_here, down_here = lax.optimization_barrier((terms, up_here, down_here))
        terms = terms + [
            apply_block(
                block_member, jnp.concatenate(up_here, axis=1), jnp.concatenate(down_here, axis=0)
            )
        ]
    tp_here = lax.axis_index("tp")
    by_target = [term.reshape(n_tp, rows_here, feature_width) for term in terms]

    def slice_for(target):
        pieces = [lax.dynamic_index_in_dim(term, target, 0, keepdims=False) for term in by_target]
        total = pieces[0]
        for piece in pieces[1:]:
            total = total + piece
        return total

    change = slice_for(tp_here)
    for shift in range(1, n_tp):
        change = change + lax.ppermute(
            slice_for((tp_here + shift) % n_tp).astype(PARTIAL_DTYPE),
            "tp",
            [(i, (i + shift) % n_tp) for i in range(n_tp)],
        ).astype(jnp.float32)
    packed = (states.astype(jnp.float32) + change).astype(jnp.bfloat16)
    spot_lanes = jnp.where(
        jnp.arange(128, dtype=jnp.int32)[None, :] == 0, packed_spot[:, None], 0
    ).astype(jnp.bfloat16)
    arrivals = lax.all_to_all(
        jnp.concatenate([packed, spot_lanes], axis=1).reshape(
            n_dev, per_learner, feature_width + 128
        ),
        ("member", "tp"),
        split_axis=0,
        concat_axis=0,
        tiled=True,
    )
    arrivals = arrivals.reshape(n_dev * per_learner, feature_width + 128)
    arrival_spots = arrivals[:, feature_width].astype(jnp.int32)
    settle = (jnp.arange(rows_here, dtype=jnp.int32)[:, None] == arrival_spots[None, :]).astype(
        jnp.bfloat16
    )
    imagined = jnp.dot(
        settle, arrivals[:, :feature_width], preferred_element_type=jnp.float32
    ).astype(jnp.bfloat16)
    policy_normed = rms_scale(imagined.astype(jnp.float32), policy_gain).astype(jnp.bfloat16)
    action = jnp.tanh(jnp.dot(policy_normed, w_policy, preferred_element_type=jnp.float32)).astype(
        jnp.bfloat16
    )
    return (imagined, action)


def solution(mesh):
    in_specs = (
        P(("rep", "member", "tp"), None),
        P(("rep", "member", "tp"), None),
        P(("rep", "member", "tp")),
        P(),
        P("member", None, "tp"),
        P("member", "tp", None),
        P(),
        P(),
    )
    out_specs = (P(("rep", "member", "tp"), None), P(("rep", "member", "tp"), None))
    return jax.shard_map(local, mesh=mesh, in_specs=in_specs, out_specs=out_specs, check_vma=False)
```

profile of v0, /device:TPU:0, one launch (start us, length us, event | category | flops | bytes accessed | tf_op | source)
XLA Modules:
  0.0 118.7 jit_solution(594228416031735746)
XLA Ops:
  7.2 0.7 and_select_fusion
  8.4 0.8 select_reduce_fusion.1
  9.6 0.8 gather_fusion
  10.6 0.8 pad_maximum_fusion
  11.8 3.0 %collective-permute-start.2 = (bf16[1024,256]{1,0:T(8,128)(2,1)S(1)}, bf16[1024,256]{1,0:T(8,128)(2,1)S(1)}, u32[]{:S(2)}, u32[]{:S(2)}) collective-permute-start(bf16[1024,256]{1,0:T(8,128)(2,1)S(1)} %dynamic-slice_bitcast_fusion), channel_id=1, source_target_pairs={{0,8},{4,12},{8,0},{12,4},{1,9},{5,13},{9,1},{13,5},{2,10},{6,14},... | collective-permute-start | bytes 1572872 | tf_op jit(solution)/shard_map/ppermute | solution.py:15
  14.8 11.9 %collective-permute-done.2 = bf16[1024,256]{1,0:T(8,128)(2,1)S(1)} collective-permute-done((bf16[1024,256]{1,0:T(8,128)(2,1)S(1)}, bf16[1024,256]{1,0:T(8,128)(2,1)S(1)}, u32[]{:S(2)}, u32[]{:S(2)}) %collective-permute-start.2) | collective-permute-done | bytes 524320 | tf_op jit(solution)/shard_map/ppermute | solution.py:15
  26.8 1.8 %collective-permute-start.6 = (bf16[256,1024]{1,0:T(8,128)(2,1)S(1)}, bf16[256,1024]{1,0:T(8,128)(2,1)}, u32[]{:S(2)}, u32[]{:S(2)}) collective-permute-start(bf16[256,1024]{1,0:T(8,128)(2,1)S(1)} %constant_dynamic-slice_fusion), channel_id=1, source_target_pairs={{0,8},{4,12},{8,0},{12,4},{1,9},{5,13},{9,1},{13,5},{2,10},{6,14},... | collective-permute-start | bytes 1572872 | tf_op jit(solution)/shard_map/ppermute | solution.py:15
  28.6 1.5 %collective-permute-start.3 = (bf16[1024,256]{1,0:T(8,128)(2,1)S(1)}, bf16[1024,256]{1,0:T(8,128)(2,1)}, u32[]{:S(2)}, u32[]{:S(2)}) collective-permute-start(bf16[1024,256]{1,0:T(8,128)(2,1)S(1)} %collective-permute-done.2), channel_id=1, source_target_pairs={{0,16},{16,0},{1,17},{17,1},{2,18},{18,2},{3,19},{19,3},{4,20},{20... | collective-permute-start | bytes 1572872 | tf_op jit(solution)/shard_map/ppermute | solution.py:21
  30.1 10.1 %collective-permute-done.6 = bf16[256,1024]{1,0:T(8,128)(2,1)} collective-permute-done((bf16[256,1024]{1,0:T(8,128)(2,1)S(1)}, bf16[256,1024]{1,0:T(8,128)(2,1)}, u32[]{:S(2)}, u32[]{:S(2)}) %collective-permute-start.6) | collective-permute-done | bytes 524320 | tf_op jit(solution)/shard_map/ppermute | solution.py:15
  40.2 1.4 %collective-permute-start.7 = (bf16[256,1024]{1,0:T(8,128)(2,1)}, bf16[256,1024]{1,0:T(8,128)(2,1)}, u32[]{:S(2)}, u32[]{:S(2)}) collective-permute-start(bf16[256,1024]{1,0:T(8,128)(2,1)} %collective-permute-done.6), channel_id=1, source_target_pairs={{0,16},{16,0},{1,17},{17,1},{2,18},{18,2},{3,19},{19,3},{4,20},{20... | collective-permute-start | bytes 1572872 | tf_op jit(solution)/shard_map/ppermute | solution.py:21
  41.6 3.1 %all-gather.2.cloned.1.call-done = bf16[512,1152]{1,0:T(8,128)(2,1)} async-done(((bf16[128,1152]{1,0:T(8,128)(2,1)}), bf16[512,1152]{1,0:T(8,128)(2,1)}) %all-gather.2.cloned.1.call-update) | async-done | bytes 1179664 | tf_op jit(solution)/shard_map/all_gather | solution.py:83
  44.7 1.1 fusion.84
  45.8 0.5 collective-permute-start.5
  46.3 7.9 %collective-permute-done.7 = bf16[256,1024]{1,0:T(8,128)(2,1)} collective-permute-done((bf16[256,1024]{1,0:T(8,128)(2,1)}, bf16[256,1024]{1,0:T(8,128)(2,1)}, u32[]{:S(2)}, u32[]{:S(2)}) %collective-permute-start.7) | collective-permute-done | bytes 524320 | tf_op jit(solution)/shard_map/ppermute | solution.py:21
  54.3 4.9 %fusion.20 = f32[512,1024]{1,0:T(8,128)S(1)} fusion(bf16[512,1024]{1,0:T(8,128)(2,1)} %collective-permute-done.1, bf16[512,1024]{1,0:T(8,128)(2,1)} %bitcast.38, bf16[1024,512]{1,0:T(8,128)(2,1)} %collective-permute-done, bf16[1024,512]{1,0:T(8,128)(2,1)} %bitcast.41, bf16[512,1152]{1,0:T(8,128)(2,1)} %all-gather.2.cloned.1.call-done, ...), kind=kOutput, calls=%fused_computation.23 | convolution fusion | flops 2161115136 | bytes 7341056 | tf_op jit(solution)/shard_map/dot_general | solution.py:97
  59.2 6.0 %fusion.32 = f32[512,1024]{1,0:T(8,128)} fusion(bf16[256,1024]{1,0:T(8,128)(2,1)} %collective-permute-done.9, bf16[256,1024]{1,0:T(8,128)(2,1)} %collective-permute-done.8, bf16[256,1024]{1,0:T(8,128)(2,1)} %collective-permute-done.7, bf16[256,1024]{1,0:T(8,128)(2,1)} %collective-permute-done.6, bf16[1024,256]{1,0:T(8,128)(2,1)} %collective-permute-done.5, ...), kind=kOutput, calls=%fused_computation.35 | convolution fusion | flops 2169503744 | bytes 7341056 | tf_op jit(solution)/shard_map/dot_general | solution.py:97
  65.3 2.3 %fusion.75 = (bf16[128,1024]{1,0:T(8,128)(2,1)S(1)}, bf16[128,1024]{1,0:T(8,128)(2,1)}, bf16[128,1024]{1,0:T(8,128)(2,1)S(1)}) fusion(f32[4,128,1024]{2,1,0:T(8,128)} %bitcast.34, s32[]{:T(128)S(6)} %select_n.91, f32[4,128,1024]{2,1,0:T(8,128)S(1)} %bitcast.32, s32[]{:T(128)S(6)} %select_n.95, s32[]{:T(128)S(6)} %select_n.93), kind=kLoop, calls=%fused_computation.77 | loop fusion | flops 786432 | bytes 3932172 | tf_op jit(solution)/shard_map/convert_element_type | solution.py:125
  67.5 3.6 %collective-permute-start.12 = (bf16[128,1024]{1,0:T(8,128)(2,1)}, bf16[128,1024]{1,0:T(8,128)(2,1)}, u32[]{:S(2)}, u32[]{:S(2)}) collective-permute-start(bf16[128,1024]{1,0:T(8,128)(2,1)} %get-tuple-element.29), channel_id=1, source_target_pairs={{0,3},{1,0},{2,1},{3,2},{4,7},{5,4},{6,5},{7,6},{8,11},{9,8},{10,9... | collective-permute-start | bytes 786440 | tf_op jit(solution)/shard_map/ppermute | solution.py:124
  71.1 1.0 collective-permute-start.10
  72.2 6.0 %collective-permute-done.12 = bf16[128,1024]{1,0:T(8,128)(2,1)} collective-permute-done((bf16[128,1024]{1,0:T(8,128)(2,1)}, bf16[128,1024]{1,0:T(8,128)(2,1)}, u32[]{:S(2)}, u32[]{:S(2)}) %collective-permute-start.12) | collective-permute-done | bytes 262176 | tf_op jit(solution)/shard_map/ppermute | solution.py:124
  78.2 16.3 %collective-permute-done.11 = bf16[128,1024]{1,0:T(8,128)(2,1)} collective-permute-done((bf16[128,1024]{1,0:T(8,128)(2,1)S(1)}, bf16[128,1024]{1,0:T(8,128)(2,1)}, u32[]{:S(2)}, u32[]{:S(2)}) %collective-permute-start.11) | collective-permute-done | bytes 262176 | tf_op jit(solution)/shard_map/ppermute | solution.py:124
  94.5 1.5 %fusion.72 = bf16[128,1024]{1,0:T(8,128)(2,1)S(1)} fusion(f32[128,1024]{1,0:T(8,128)S(1)} %get-tuple-element.36, bf16[128,1024]{1,0:T(8,128)(2,1)} %collective-permute-done.12, bf16[128,1024]{1,0:T(8,128)(2,1)} %collective-permute-done.11, bf16[128,1024]{1,0:T(8,128)(2,1)} %collective-permute-done.10, f32[4,128,1024]{2,1,0:T(8,128)} %bitcast.35, ...), kind=kLoop, calls=%fused_computation.64 | loop fusion | flops 1179648 | bytes 2621444 | tf_op jit(solution)/shard_map/convert_element_type | solution.py:129
  96.0 14.5 %all_to_all.5 = bf16[16,8,1152]{2,1,0:T(8,128)(2,1)S(1)} all-to-all(bf16[16,8,1152]{2,1,0:T(8,128)(2,1)S(1)} %maximum_bitcast_fusion), channel_id=1, replica_groups=mesh['rep'=2,'member'=4,'tp'=4] {'member','tp'}, dimensions={0} | all-to-all | bytes 589824 | tf_op jit(solution)/shard_map/all_to_all | solution.py:133
  111.0 0.9 fusion.41
  (47 shorter events, 2.1 us)
Async XLA Ops:
  7.2 2.0 %copy-start = (bf16[128,1024]{1,0:T(8,128)(2,1)S(1)}, bf16[128,1024]{1,0:T(8,128)(2,1)}, u32[]{:S(2)}) copy-start(bf16[128,1024]{1,0:T(8,128)(2,1)} %param.8) | copy-start | bytes 786436
  7.2 2.4 %copy-start.1 = (f32[2,1024]{1,0:T(2,128)S(1)}, f32[2,1024]{1,0:T(2,128)}, u32[]{:S(2)}) copy-start(f32[2,1024]{1,0:T(2,128)} %param.11) | copy-start | bytes 24580
  7.2 37.5 %all-gather.2.cloned.1.call-start = ((), (), s32[]{:S(2)}) async-start(), calls=%async_computation.1 | async-start | bytes 1474560 | tf_op jit(solution)/shard_map/all_gather | solution.py:83
  10.4 1.3 %copy-start.3 = (bf16[1,1024,512]{2,1,0:T(8,128)(2,1)S(1)}, bf16[1,1024,512]{2,1,0:T(8,128)(2,1)}, u32[]{:S(2)}) copy-start(bf16[1,1024,512]{2,1,0:T(8,128)(2,1)} %param.12) | copy-start | bytes 3145732
  10.4 4.4 %copy-start.2 = (bf16[1,512,1024]{2,1,0:T(8,128)(2,1)S(1)}, bf16[1,512,1024]{2,1,0:T(8,128)(2,1)}, u32[]{:S(2)}) copy-start(bf16[1,512,1024]{2,1,0:T(8,128)(2,1)} %param.13) | copy-start | bytes 3145732
  11.8 15.0 %collective-permute-start.2 = (bf16[1024,256]{1,0:T(8,128)(2,1)S(1)}, bf16[1024,256]{1,0:T(8,128)(2,1)S(1)}, u32[]{:S(2)}, u32[]{:S(2)}) collective-permute-start(bf16[1024,256]{1,0:T(8,128)(2,1)S(1)} %dynamic-slice_bitcast_fusion), channel_id=1, source_target_pairs={{0,8},{4,12},{8,0},{12,4},{1,9},{5,13},{9,1},{13,5},{2,10},{6,14},... | collective-permute-start | bytes 1572872 | tf_op jit(solution)/shard_map/ppermute | solution.py:15
  14.8 30.9 %collective-permute-start.1 = (bf16[512,1024]{1,0:T(8,128)(2,1)S(1)}, bf16[512,1024]{1,0:T(8,128)(2,1)}, u32[]{:S(2)}, u32[]{:S(2)}) collective-permute-start(bf16[512,1024]{1,0:T(8,128)(2,1)S(1)} %bitcast.39), channel_id=1, source_target_pairs={{0,4},{4,0},{8,12},{12,8},{1,5},{5,1},{9,13},{13,9},{2,6},{6,2},{1... | collective-permute-start | bytes 3145736 | tf_op jit(solution)/shard_map/ppermute | solution.py:10
  26.8 13.4 %collective-permute-start.6 = (bf16[256,1024]{1,0:T(8,128)(2,1)S(1)}, bf16[256,1024]{1,0:T(8,128)(2,1)}, u32[]{:S(2)}, u32[]{:S(2)}) collective-permute-start(bf16[256,1024]{1,0:T(8,128)(2,1)S(1)} %constant_dynamic-slice_fusion), channel_id=1, source_target_pairs={{0,8},{4,12},{8,0},{12,4},{1,9},{5,13},{9,1},{13,5},{2,10},{6,14},... | collective-permute-start | bytes 1572872 | tf_op jit(solution)/shard_map/ppermute | solution.py:15
  28.6 25.7 %collective-permute-start = (bf16[1024,512]{1,0:T(8,128)(2,1)S(1)}, bf16[1024,512]{1,0:T(8,128)(2,1)}, u32[]{:S(2)}, u32[]{:S(2)}) collective-permute-start(bf16[1024,512]{1,0:T(8,128)(2,1)S(1)} %bitcast.42), channel_id=1, source_target_pairs={{0,4},{4,0},{8,12},{12,8},{1,5},{5,1},{9,13},{13,9},{2,6},{6,2},{1... | collective-permute-start | bytes 3145736 | tf_op jit(solution)/shard_map/ppermute | solution.py:10
  28.6 17.2 %collective-permute-start.3 = (bf16[1024,256]{1,0:T(8,128)(2,1)S(1)}, bf16[1024,256]{1,0:T(8,128)(2,1)}, u32[]{:S(2)}, u32[]{:S(2)}) collective-permute-start(bf16[1024,256]{1,0:T(8,128)(2,1)S(1)} %collective-permute-done.2), channel_id=1, source_target_pairs={{0,16},{16,0},{1,17},{17,1},{2,18},{18,2},{3,19},{19,3},{4,20},{20... | collective-permute-start | bytes 1572872 | tf_op jit(solution)/shard_map/ppermute | solution.py:21
  40.2 14.1 %collective-permute-start.7 = (bf16[256,1024]{1,0:T(8,128)(2,1)}, bf16[256,1024]{1,0:T(8,128)(2,1)}, u32[]{:S(2)}, u32[]{:S(2)}) collective-permute-start(bf16[256,1024]{1,0:T(8,128)(2,1)} %collective-permute-done.6), channel_id=1, source_target_pairs={{0,16},{16,0},{1,17},{17,1},{2,18},{18,2},{3,19},{19,3},{4,20},{20... | collective-permute-start | bytes 1572872 | tf_op jit(solution)/shard_map/ppermute | solution.py:21
  41.6 17.6 %collective-permute-start.4 = (bf16[1024,256]{1,0:T(8,128)(2,1)S(1)}, bf16[1024,256]{1,0:T(8,128)(2,1)}, u32[]{:S(2)}, u32[]{:S(2)}) collective-permute-start(bf16[1024,256]{1,0:T(8,128)(2,1)S(1)} %collective-permute-done.2), channel_id=1, source_target_pairs={{0,4},{4,0},{8,12},{12,8},{1,5},{5,1},{9,13},{13,9},{2,6},{6,2},{1... | collective-permute-start | bytes 1572872 | tf_op jit(solution)/shard_map/ppermute | solution.py:10
  45.8 13.5 %collective-permute-start.8 = (bf16[256,1024]{1,0:T(8,128)(2,1)}, bf16[256,1024]{1,0:T(8,128)(2,1)}, u32[]{:S(2)}, u32[]{:S(2)}) collective-permute-start(bf16[256,1024]{1,0:T(8,128)(2,1)} %collective-permute-done.6), channel_id=1, source_target_pairs={{0,4},{4,0},{8,12},{12,8},{1,5},{5,1},{9,13},{13,9},{2,6},{6,2},{1... | collective-permute-start | bytes 1572872 | tf_op jit(solution)/shard_map/ppermute | solution.py:10
  45.8 13.4 %collective-permute-start.5 = (bf16[1024,256]{1,0:T(8,128)(2,1)}, bf16[1024,256]{1,0:T(8,128)(2,1)}, u32[]{:S(2)}, u32[]{:S(2)}) collective-permute-start(bf16[1024,256]{1,0:T(8,128)(2,1)} %collective-permute-done.3), channel_id=1, source_target_pairs={{0,4},{4,0},{8,12},{12,8},{1,5},{5,1},{9,13},{13,9},{2,6},{6,2},{1... | collective-permute-start | bytes 1572872 | tf_op jit(solution)/shard_map/ppermute | solution.py:10
  54.3 5.0 %collective-permute-start.9 = (bf16[256,1024]{1,0:T(8,128)(2,1)}, bf16[256,1024]{1,0:T(8,128)(2,1)}, u32[]{:S(2)}, u32[]{:S(2)}) collective-permute-start(bf16[256,1024]{1,0:T(8,128)(2,1)} %collective-permute-done.7), channel_id=1, source_target_pairs={{0,4},{4,0},{8,12},{12,8},{1,5},{5,1},{9,13},{13,9},{2,6},{6,2},{1... | collective-permute-start | bytes 1572872 | tf_op jit(solution)/shard_map/ppermute | solution.py:10
  67.5 10.6 %collective-permute-start.12 = (bf16[128,1024]{1,0:T(8,128)(2,1)}, bf16[128,1024]{1,0:T(8,128)(2,1)}, u32[]{:S(2)}, u32[]{:S(2)}) collective-permute-start(bf16[128,1024]{1,0:T(8,128)(2,1)} %get-tuple-element.29), channel_id=1, source_target_pairs={{0,3},{1,0},{2,1},{3,2},{4,7},{5,4},{6,5},{7,6},{8,11},{9,8},{10,9... | collective-permute-start | bytes 786440 | tf_op jit(solution)/shard_map/ppermute | solution.py:124
  71.1 23.3 %collective-permute-start.11 = (bf16[128,1024]{1,0:T(8,128)(2,1)S(1)}, bf16[128,1024]{1,0:T(8,128)(2,1)}, u32[]{:S(2)}, u32[]{:S(2)}) collective-permute-start(bf16[128,1024]{1,0:T(8,128)(2,1)S(1)} %get-tuple-element.30), channel_id=1, source_target_pairs={{0,2},{1,3},{2,0},{3,1},{4,6},{5,7},{6,4},{7,5},{8,10},{9,11},{10,... | collective-permute-start | bytes 786440 | tf_op jit(solution)/shard_map/ppermute | solution.py:124
  71.1 23.3 %collective-permute-start.10 = (bf16[128,1024]{1,0:T(8,128)(2,1)S(1)}, bf16[128,1024]{1,0:T(8,128)(2,1)}, u32[]{:S(2)}, u32[]{:S(2)}) collective-permute-start(bf16[128,1024]{1,0:T(8,128)(2,1)S(1)} %get-tuple-element.28), channel_id=1, source_target_pairs={{0,1},{1,2},{2,3},{3,0},{4,5},{5,6},{6,7},{7,4},{8,9},{9,10},{10,1... | collective-permute-start | bytes 786440 | tf_op jit(solution)/shard_map/ppermute | solution.py:124
  72.2 38.8 %copy-start.4 = (bf16[1024,128]{1,0:T(8,128)(2,1)S(1)}, bf16[1024,128]{1,0:T(8,128)(2,1)}, u32[]{:S(2)}) copy-start(bf16[1024,128]{1,0:T(8,128)(2,1)} %param.15) | copy-start | bytes 786436
  72.2 38.8 %copy-start.5 = (f32[1024]{0:T(1024)S(1)}, f32[1024]{0:T(1024)}, u32[]{:S(2)}) copy-start(f32[1024]{0:T(1024)} %param.14) | copy-start | bytes 12292
  110.9 1.0 copy-start.6
Sparse Core Ops, SparseCore 0:
  11.5 33.1 all-gather.1
where the time goes:
time: 119 us
  waiting for transfers between devices  55.4 us (47%)
  blocking collectives  14.5 us (12%)
  between operations  14.3 us (12%)
  starting transfers between devices  12.9 us (11%)
  matrix products  12.5 us (11%)
  other arithmetic  7.9 us (7%)
  local copies, waits for them, and re-layouts  1.27 us (1%)
    ppermute x3, waiting for transfers between devices, local(): lax.ppermute(slice_for((tp_here + shift) % n_tp).astype(PARTIAL_DTYPE), '...  22.3 us
    ppermute x2, waiting for transfers between devices, from_chip_behind(): lax.ppermute(value, axis, [(i, (i + 2 * chips_back) % size) for i in rang...  22 us
    all_to_all x1, blocking collectives, local(): lax.all_to_all(jnp.concatenate([packed, spot_lanes], axis=1).reshape(n_de...  14.5 us
    dot_general x2, matrix products, apply_block(): return jnp.dot(hidden, down_here, preferred_element_type=jnp.float32)  10.9 us
    ppermute x2, waiting for transfers between devices, swap_parts(): lax.ppermute(value, 'rep', [(i, (i + step) % n_rep) for i in range(n_rep)])  7.94 us
    ppermute x2, starting transfers between devices, from_chip_behind(): lax.ppermute(value, axis, [(i, (i + 2 * chips_back) % size) for i in rang...  4.84 us
    ppermute x3, starting transfers between devices, local(): lax.ppermute(slice_for((tp_here + shift) % n_tp).astype(PARTIAL_DTYPE), '...  4.61 us
    all_gather x1, waiting for transfers between devices, local(): lax.all_gather(jnp.concatenate([normed, member_lanes], axis=1), 'tp', axi...  3.1 us
  transfers between devices with their start and end apart: 14, of which 6 were waited for; matrix products, arithmetic and copies ran while one was open for 5% of the time, Pallas kernels for 0%

commit v1 on v0

--- a/solution.py
+++ b/solution.py
@@ -4,6 +4,18 @@
 from jax.sharding import PartitionSpec as P
 
 PARTIAL_DTYPE = jnp.bfloat16
+
+
+def doubled_up(x, axis, dim):
+    ways, here, step = (lax.axis_size(axis), lax.axis_index(axis), x.shape[dim])
+    line, have = (x, 1)
+    while have < ways:
+        line = jnp.concatenate(
+            [line, lax.ppermute(line, axis, [(d, (d - have) % ways) for d in range(ways)])],
+            axis=dim,
+        )
+        have = 2 * have
+    return jnp.roll(line, here * step, axis=dim)
 
 
 def from_partner(value, axis, distance):
@@ -80,9 +92,7 @@
     member_lanes = jnp.where(
         jnp.arange(128, dtype=jnp.int32)[None, :] == 0, member[:, None], 0
     ).astype(jnp.bfloat16)
-    gathered = lax.all_gather(
-        jnp.concatenate([normed, member_lanes], axis=1), "tp", axis=0, tiled=True
-    )
+    gathered = doubled_up(jnp.concatenate([normed, member_lanes], axis=1), "tp", 0)
     gathered_rows = gathered[:, :feature_width]
     gathered_member = gathered[:, feature_width].astype(jnp.int32)
 

time: 119 us -> 117 us (0.983)
  between operations: 14.3 us -> 0.86 us
  local copies, waits for them, and re-layouts: 1.27 us -> 7.01 us
  starting transfers between devices: 12.9 us -> 16.8 us
  blocking collectives: 14.5 us -> 16.1 us
    ppermute x0 -> x2, waiting for transfers between devices: none -> 17 us  [doubled_up(): lax.ppermute(line, axis, [(d, (d - have) % ways) for d in range(ways)])]
    ppermute x2, waiting for transfers between devices: 22 us -> 6.68 us  [from_chip_behind(): lax.ppermute(value, axis, [(i, (i + 2 * chips_back) % size) for i in rang...]
    ppermute x0 -> x2, starting transfers between devices: none -> 6.59 us  [doubled_up(): lax.ppermute(line, axis, [(d, (d - have) % ways) for d in range(ways)])]
    all_gather x1 -> x0, waiting for transfers between devices: 3.1 us -> none  [local(): lax.all_gather(jnp.concatenate([normed, member_lanes], axis=1), 'tp', axi...]
    unnamed x14 -> x17, local copies, waits for them, and re-layouts: 0.42 us -> 3.19 us
    ppermute x3, starting transfers between devices: 4.61 us -> 2.92 us  [local(): lax.ppermute(slice_for((tp_here + shift) % n_tp).astype(PARTIAL_DTYPE), '...]
    ppermute x2, starting transfers between devices: 4.84 us -> 3.17 us  [from_chip_behind(): lax.ppermute(value, axis, [(i, (i + 2 * chips_back) % size) for i in rang...]
    all_to_all x1, blocking collectives: 14.5 us -> 16.1 us  [local(): lax.all_to_all(jnp.concatenate([packed, spot_lanes], axis=1).reshape(n_de...]
  transfers between devices with their start and end apart: 14 -> 15, of which waited for: 6 -> 6; matrix products, arithmetic and copies ran while one was open for 5% -> 11% of each run, Pallas kernels for 0% -> 0%
where the time goes in v1:
time: 117 us
  waiting for transfers between devices  54.7 us (47%)
  starting transfers between devices  16.8 us (14%)
  blocking collectives  16.1 us (14%)
  matrix products  12.5 us (11%)
  other arithmetic  8.72 us (7%)
  local copies, waits for them, and re-layouts  7.01 us (6%)
    ppermute x3, waiting for transfers between devices, local(): lax.ppermute(slice_for((tp_here + shift) % n_tp).astype(PARTIAL_DTYPE), '...  22 us
    ppermute x2, waiting for transfers between devices, doubled_up(): lax.ppermute(line, axis, [(d, (d - have) % ways) for d in range(ways)])  17 us
    all_to_all x1, blocking collectives, local(): lax.all_to_all(jnp.concatenate([packed, spot_lanes], axis=1).reshape(n_de...  16.1 us
    dot_general x2, matrix products, apply_block(): return jnp.dot(hidden, down_here, preferred_element_type=jnp.float32)  11 us
    ppermute x2, waiting for transfers between devices, swap_parts(): lax.ppermute(value, 'rep', [(i, (i + step) % n_rep) for i in range(n_rep)])  9.1 us
    ppermute x2, waiting for transfers between devices, from_chip_behind(): lax.ppermute(value, axis, [(i, (i + 2 * chips_back) % size) for i in rang...  6.68 us
    ppermute x2, starting transfers between devices, doubled_up(): lax.ppermute(line, axis, [(d, (d - have) % ways) for d in range(ways)])  6.59 us
    unnamed x17, local copies, waits for them, and re-layouts  3.19 us
  transfers between devices with their start and end apart: 15, of which 6 were waited for; matrix products, arithmetic and copies ran while one was open for 11% of the time, Pallas kernels for 0%

profile of v1, /device:TPU:0, one launch (start us, length us, event | category | flops | bytes accessed | tf_op | source)
XLA Modules:
  0.0 116.7 jit_solution(2876991393173257868)
XLA Ops:
  4.7 5.1 %collective-permute-start = (bf16[128,1152]{1,0:T(8,128)(2,1)S(1)}, bf16[128,1152]{1,0:T(8,128)(2,1)S(1)}, u32[]{:S(2)}, u32[]{:S(2)}) collective-permute-start(bf16[128,1152]{1,0:T(8,128)(2,1)S(1)} %get-tuple-element.31), channel_id=1, source_target_pairs={{0,3},{1,0},{2,1},{3,2},{4,7},{5,4},{6,5},{7,6},{8,11},{9,8},{10,9... | collective-permute-start | bytes 884744 | tf_op jit(solution)/shard_map/ppermute | solution.py:14
  9.8 1.1 dynamic-slice_bitcast_fusion
  10.9 1.6 %collective-permute-start.4 = (bf16[1024,256]{1,0:T(8,128)(2,1)S(1)}, bf16[1024,256]{1,0:T(8,128)(2,1)S(1)}, u32[]{:S(2)}, u32[]{:S(2)}) collective-permute-start(bf16[1024,256]{1,0:T(8,128)(2,1)S(1)} %dynamic-slice_bitcast_fusion), channel_id=1, source_target_pairs={{0,8},{4,12},{8,0},{12,4},{1,9},{5,13},{9,1},{13,5},{2,10},{6,14},... | collective-permute-start | bytes 1572872 | tf_op jit(solution)/shard_map/ppermute | solution.py:27
  12.5 3.6 %collective-permute-done = bf16[128,1152]{1,0:T(8,128)(2,1)S(1)} collective-permute-done((bf16[128,1152]{1,0:T(8,128)(2,1)S(1)}, bf16[128,1152]{1,0:T(8,128)(2,1)S(1)}, u32[]{:S(2)}, u32[]{:S(2)}) %collective-permute-start) | collective-permute-done | bytes 294944 | tf_op jit(solution)/shard_map/ppermute | solution.py:14
  16.1 1.5 %collective-permute-start.1 = (bf16[256,1152]{1,0:T(8,128)(2,1)S(1)}, bf16[256,1152]{1,0:T(8,128)(2,1)S(1)}, u32[]{:S(2)}, u32[]{:S(2)}) collective-permute-start(bf16[256,1152]{1,0:T(8,128)(2,1)S(1)} %pad_maximum_fusion), channel_id=1, source_target_pairs={{0,2},{1,3},{2,0},{3,1},{4,6},{5,7},{6,4},{7,5},{8,10},{9,11},{10,... | collective-permute-start | bytes 1769480 | tf_op jit(solution)/shard_map/ppermute | solution.py:14
  17.6 6.7 %collective-permute-done.4 = bf16[1024,256]{1,0:T(8,128)(2,1)S(1)} collective-permute-done((bf16[1024,256]{1,0:T(8,128)(2,1)S(1)}, bf16[1024,256]{1,0:T(8,128)(2,1)S(1)}, u32[]{:S(2)}, u32[]{:S(2)}) %collective-permute-start.4) | collective-permute-done | bytes 524320 | tf_op jit(solution)/shard_map/ppermute | solution.py:27
  25.1 1.1 constant_dynamic-slice_fusion
  26.2 1.6 %collective-permute-start.8 = (bf16[256,1024]{1,0:T(8,128)(2,1)S(1)}, bf16[256,1024]{1,0:T(8,128)(2,1)}, u32[]{:S(2)}, u32[]{:S(2)}) collective-permute-start(bf16[256,1024]{1,0:T(8,128)(2,1)S(1)} %constant_dynamic-slice_fusion), channel_id=1, source_target_pairs={{0,8},{4,12},{8,0},{12,4},{1,9},{5,13},{9,1},{13,5},{2,10},{6,14},... | collective-permute-start | bytes 1572872 | tf_op jit(solution)/shard_map/ppermute | solution.py:27
  29.0 1.5 %collective-permute-start.5 = (bf16[1024,256]{1,0:T(8,128)(2,1)}, bf16[1024,256]{1,0:T(8,128)(2,1)}, u32[]{:S(2)}, u32[]{:S(2)}) collective-permute-start(bf16[1024,256]{1,0:T(8,128)(2,1)} %copy-done.2), channel_id=1, source_target_pairs={{0,16},{16,0},{1,17},{17,1},{2,18},{18,2},{3,19},{19,3},{4,20},{20... | collective-permute-start | bytes 1572872 | tf_op jit(solution)/shard_map/ppermute | solution.py:33
  30.5 13.4 %collective-permute-done.1 = bf16[256,1152]{1,0:T(8,128)(2,1)S(1)} collective-permute-done((bf16[256,1152]{1,0:T(8,128)(2,1)S(1)}, bf16[256,1152]{1,0:T(8,128)(2,1)S(1)}, u32[]{:S(2)}, u32[]{:S(2)}) %collective-permute-start.1) | collective-permute-done | bytes 589856 | tf_op jit(solution)/shard_map/ppermute | solution.py:14
  43.9 0.9 constant_dynamic-update-slice_fusion.3
  44.8 1.5 %collective-permute-start.9 = (bf16[256,1024]{1,0:T(8,128)(2,1)}, bf16[256,1024]{1,0:T(8,128)(2,1)}, u32[]{:S(2)}, u32[]{:S(2)}) collective-permute-start(bf16[256,1024]{1,0:T(8,128)(2,1)} %collective-permute-done.8), channel_id=1, source_target_pairs={{0,16},{16,0},{1,17},{17,1},{2,18},{18,2},{3,19},{19,3},{4,20},{20... | collective-permute-start | bytes 1572872 | tf_op jit(solution)/shard_map/ppermute | solution.py:33
  47.8 0.9 constant_dynamic-update-slice_fusion
  48.7 1.1 fusion.84
  50.3 9.1 %collective-permute-done.9 = bf16[256,1024]{1,0:T(8,128)(2,1)} collective-permute-done((bf16[256,1024]{1,0:T(8,128)(2,1)}, bf16[256,1024]{1,0:T(8,128)(2,1)}, u32[]{:S(2)}, u32[]{:S(2)}) %collective-permute-start.9) | collective-permute-done | bytes 524320 | tf_op jit(solution)/shard_map/ppermute | solution.py:33
  59.5 5.0 %fusion.20 = f32[512,1024]{1,0:T(8,128)S(1)} fusion(bf16[512,1024]{1,0:T(8,128)(2,1)} %collective-permute-done.3, bf16[512,1024]{1,0:T(8,128)(2,1)} %bitcast.40, bf16[1024,512]{1,0:T(8,128)(2,1)} %collective-permute-done.2, bf16[1024,512]{1,0:T(8,128)(2,1)} %bitcast.42, bf16[1024,1152]{1,0:T(8,128)(2,1)} %constant_dynamic-update-slice_fusion, ...), kind=kOutput, calls=%fused_computation.23 | convolution fusion | flops 2161115136 | bytes 7341060 | tf_op jit(solution)/shard_map/dot_general | solution.py:107
  64.5 6.0 %fusion.32 = f32[512,1024]{1,0:T(8,128)} fusion(bf16[256,1024]{1,0:T(8,128)(2,1)} %collective-permute-done.11, bf16[256,1024]{1,0:T(8,128)(2,1)} %collective-permute-done.10, bf16[256,1024]{1,0:T(8,128)(2,1)} %collective-permute-done.9, bf16[256,1024]{1,0:T(8,128)(2,1)} %collective-permute-done.8, bf16[512]{0:T(512)(128)(2,1)S(1)} %get-tuple-element.24, ...), kind=kOutput, calls=%fused_computation.35 | convolution fusion | flops 2169503744 | bytes 7341060 | tf_op jit(solution)/shard_map/dot_general | solution.py:107
  70.5 2.3 %fusion.75 = (bf16[128,1024]{1,0:T(8,128)(2,1)S(1)}, bf16[128,1024]{1,0:T(8,128)(2,1)}, bf16[128,1024]{1,0:T(8,128)(2,1)S(1)}) fusion(f32[4,128,1024]{2,1,0:T(8,128)} %bitcast.34, s32[]{:T(128)S(6)} %select_n.105, f32[4,128,1024]{2,1,0:T(8,128)S(1)} %bitcast.32, s32[]{:T(128)S(6)} %select_n.109, s32[]{:T(128)S(6)} %select_n.107), kind=kLoop, calls=%fused_computation.78 | loop fusion | flops 786432 | bytes 3932172 | tf_op jit(solution)/shard_map/convert_element_type | solution.py:135
  72.8 2.4 %collective-permute-start.14 = (bf16[128,1024]{1,0:T(8,128)(2,1)}, bf16[128,1024]{1,0:T(8,128)(2,1)}, u32[]{:S(2)}, u32[]{:S(2)}) collective-permute-start(bf16[128,1024]{1,0:T(8,128)(2,1)} %get-tuple-element.29), channel_id=1, source_target_pairs={{0,3},{1,0},{2,1},{3,2},{4,7},{5,4},{6,5},{7,6},{8,11},{9,8},{10,9... | collective-permute-start | bytes 786440 | tf_op jit(solution)/shard_map/ppermute | solution.py:134
  75.7 7.8 %collective-permute-done.14 = bf16[128,1024]{1,0:T(8,128)(2,1)} collective-permute-done((bf16[128,1024]{1,0:T(8,128)(2,1)}, bf16[128,1024]{1,0:T(8,128)(2,1)}, u32[]{:S(2)}, u32[]{:S(2)}) %collective-permute-start.14) | collective-permute-done | bytes 262176 | tf_op jit(solution)/shard_map/ppermute | solution.py:134
  83.5 14.2 %collective-permute-done.13 = bf16[128,1024]{1,0:T(8,128)(2,1)} collective-permute-done((bf16[128,1024]{1,0:T(8,128)(2,1)S(1)}, bf16[128,1024]{1,0:T(8,128)(2,1)}, u32[]{:S(2)}, u32[]{:S(2)}) %collective-permute-start.13) | collective-permute-done | bytes 262176 | tf_op jit(solution)/shard_map/ppermute | solution.py:134
  97.7 1.5 %fusion.64 = bf16[128,1024]{1,0:T(8,128)(2,1)S(1)} fusion(f32[128,1024]{1,0:T(8,128)S(1)} %get-tuple-element.38, bf16[128,1024]{1,0:T(8,128)(2,1)} %collective-permute-done.14, bf16[128,1024]{1,0:T(8,128)(2,1)} %collective-permute-done.13, bf16[128,1024]{1,0:T(8,128)(2,1)} %collective-permute-done.12, f32[4,128,1024]{2,1,0:T(8,128)} %bitcast.35, ...), kind=kLoop, calls=%fused_computation.65 | loop fusion | flops 1179648 | bytes 2621444 | tf_op jit(solution)/shard_map/convert_element_type | solution.py:139
  99.2 16.1 %all_to_all.5 = bf16[16,8,1152]{2,1,0:T(8,128)(2,1)S(1)} all-to-all(bf16[16,8,1152]{2,1,0:T(8,128)(2,1)S(1)} %maximum_bitcast_fusion), channel_id=1, replica_groups=mesh['rep'=2,'member'=4,'tp'=4] {'member','tp'}, dimensions={0} | all-to-all | bytes 589824 | tf_op jit(solution)/shard_map/all_to_all | solution.py:143
  115.8 0.9 fusion.41
  (54 shorter events, 9.2 us)
Async XLA Ops:
  0.6 2.0 %copy-start = (bf16[128,1024]{1,0:T(8,128)(2,1)S(1)}, bf16[128,1024]{1,0:T(8,128)(2,1)}, u32[]{:S(2)}) copy-start(bf16[128,1024]{1,0:T(8,128)(2,1)} %param.8) | copy-start | bytes 786436
  0.6 2.4 %copy-start.1 = (f32[2,1024]{1,0:T(2,128)S(1)}, f32[2,1024]{1,0:T(2,128)}, u32[]{:S(2)}) copy-start(f32[2,1024]{1,0:T(2,128)} %param.11) | copy-start | bytes 24580
  4.7 11.3 %collective-permute-start = (bf16[128,1152]{1,0:T(8,128)(2,1)S(1)}, bf16[128,1152]{1,0:T(8,128)(2,1)S(1)}, u32[]{:S(2)}, u32[]{:S(2)}) collective-permute-start(bf16[128,1152]{1,0:T(8,128)(2,1)S(1)} %get-tuple-element.31), channel_id=1, source_target_pairs={{0,3},{1,0},{2,1},{3,2},{4,7},{5,4},{6,5},{7,6},{8,11},{9,8},{10,9... | collective-permute-start | bytes 884744 | tf_op jit(solution)/shard_map/ppermute | solution.py:14
  10.9 13.4 %collective-permute-start.4 = (bf16[1024,256]{1,0:T(8,128)(2,1)S(1)}, bf16[1024,256]{1,0:T(8,128)(2,1)S(1)}, u32[]{:S(2)}, u32[]{:S(2)}) collective-permute-start(bf16[1024,256]{1,0:T(8,128)(2,1)S(1)} %dynamic-slice_bitcast_fusion), channel_id=1, source_target_pairs={{0,8},{4,12},{8,0},{12,4},{1,9},{5,13},{9,1},{13,5},{2,10},{6,14},... | collective-permute-start | bytes 1572872 | tf_op jit(solution)/shard_map/ppermute | solution.py:27
  16.1 27.8 %collective-permute-start.1 = (bf16[256,1152]{1,0:T(8,128)(2,1)S(1)}, bf16[256,1152]{1,0:T(8,128)(2,1)S(1)}, u32[]{:S(2)}, u32[]{:S(2)}) collective-permute-start(bf16[256,1152]{1,0:T(8,128)(2,1)S(1)} %pad_maximum_fusion), channel_id=1, source_target_pairs={{0,2},{1,3},{2,0},{3,1},{4,6},{5,7},{6,4},{7,5},{8,10},{9,11},{10,... | collective-permute-start | bytes 1769480 | tf_op jit(solution)/shard_map/ppermute | solution.py:14
  24.3 0.8 copy-start.2
  26.2 18.6 %collective-permute-start.8 = (bf16[256,1024]{1,0:T(8,128)(2,1)S(1)}, bf16[256,1024]{1,0:T(8,128)(2,1)}, u32[]{:S(2)}, u32[]{:S(2)}) collective-permute-start(bf16[256,1024]{1,0:T(8,128)(2,1)S(1)} %constant_dynamic-slice_fusion), channel_id=1, source_target_pairs={{0,8},{4,12},{8,0},{12,4},{1,9},{5,13},{9,1},{13,5},{2,10},{6,14},... | collective-permute-start | bytes 1572872 | tf_op jit(solution)/shard_map/ppermute | solution.py:27
  27.8 22.0 %collective-permute-start.3 = (bf16[512,1024]{1,0:T(8,128)(2,1)}, bf16[512,1024]{1,0:T(8,128)(2,1)}, u32[]{:S(2)}, u32[]{:S(2)}) collective-permute-start(bf16[512,1024]{1,0:T(8,128)(2,1)} %bitcast.39), channel_id=1, source_target_pairs={{0,4},{4,0},{8,12},{12,8},{1,5},{5,1},{9,13},{13,9},{2,6},{6,2},{1... | collective-permute-start | bytes 3145736 | tf_op jit(solution)/shard_map/ppermute | solution.py:22
  27.8 31.7 %collective-permute-start.2 = (bf16[1024,512]{1,0:T(8,128)(2,1)}, bf16[1024,512]{1,0:T(8,128)(2,1)}, u32[]{:S(2)}, u32[]{:S(2)}) collective-permute-start(bf16[1024,512]{1,0:T(8,128)(2,1)} %bitcast.41), channel_id=1, source_target_pairs={{0,4},{4,0},{8,12},{12,8},{1,5},{5,1},{9,13},{13,9},{2,6},{6,2},{1... | collective-permute-start | bytes 3145736 | tf_op jit(solution)/shard_map/ppermute | solution.py:22
  29.0 21.0 %collective-permute-start.5 = (bf16[1024,256]{1,0:T(8,128)(2,1)}, bf16[1024,256]{1,0:T(8,128)(2,1)}, u32[]{:S(2)}, u32[]{:S(2)}) collective-permute-start(bf16[1024,256]{1,0:T(8,128)(2,1)} %copy-done.2), channel_id=1, source_target_pairs={{0,16},{16,0},{1,17},{17,1},{2,18},{18,2},{3,19},{19,3},{4,20},{20... | collective-permute-start | bytes 1572872 | tf_op jit(solution)/shard_map/ppermute | solution.py:33
  43.9 20.5 %collective-permute-start.6 = (bf16[1024,256]{1,0:T(8,128)(2,1)}, bf16[1024,256]{1,0:T(8,128)(2,1)}, u32[]{:S(2)}, u32[]{:S(2)}) collective-permute-start(bf16[1024,256]{1,0:T(8,128)(2,1)} %copy-done.2), channel_id=1, source_target_pairs={{0,4},{4,0},{8,12},{12,8},{1,5},{5,1},{9,13},{13,9},{2,6},{6,2},{1... | collective-permute-start | bytes 1572872 | tf_op jit(solution)/shard_map/ppermute | solution.py:22
  44.8 14.7 %collective-permute-start.9 = (bf16[256,1024]{1,0:T(8,128)(2,1)}, bf16[256,1024]{1,0:T(8,128)(2,1)}, u32[]{:S(2)}, u32[]{:S(2)}) collective-permute-start(bf16[256,1024]{1,0:T(8,128)(2,1)} %collective-permute-done.8), channel_id=1, source_target_pairs={{0,16},{16,0},{1,17},{17,1},{2,18},{18,2},{3,19},{19,3},{4,20},{20... | collective-permute-start | bytes 1572872 | tf_op jit(solution)/shard_map/ppermute | solution.py:33
  49.8 14.7 %collective-permute-start.10 = (bf16[256,1024]{1,0:T(8,128)(2,1)}, bf16[256,1024]{1,0:T(8,128)(2,1)}, u32[]{:S(2)}, u32[]{:S(2)}) collective-permute-start(bf16[256,1024]{1,0:T(8,128)(2,1)} %collective-permute-done.8), channel_id=1, source_target_pairs={{0,4},{4,0},{8,12},{12,8},{1,5},{5,1},{9,13},{13,9},{2,6},{6,2},{1... | collective-permute-start | bytes 1572872 | tf_op jit(solution)/shard_map/ppermute | solution.py:22
  50.1 14.4 %collective-permute-start.7 = (bf16[1024,256]{1,0:T(8,128)(2,1)}, bf16[1024,256]{1,0:T(8,128)(2,1)}, u32[]{:S(2)}, u32[]{:S(2)}) collective-permute-start(bf16[1024,256]{1,0:T(8,128)(2,1)} %collective-permute-done.5), channel_id=1, source_target_pairs={{0,4},{4,0},{8,12},{12,8},{1,5},{5,1},{9,13},{13,9},{2,6},{6,2},{1... | collective-permute-start | bytes 1572872 | tf_op jit(solution)/shard_map/ppermute | solution.py:22
  59.4 5.0 %collective-permute-start.11 = (bf16[256,1024]{1,0:T(8,128)(2,1)}, bf16[256,1024]{1,0:T(8,128)(2,1)}, u32[]{:S(2)}, u32[]{:S(2)}) collective-permute-start(bf16[256,1024]{1,0:T(8,128)(2,1)} %collective-permute-done.9), channel_id=1, source_target_pairs={{0,4},{4,0},{8,12},{12,8},{1,5},{5,1},{9,13},{13,9},{2,6},{6,2},{1... | collective-permute-start | bytes 1572872 | tf_op jit(solution)/shard_map/ppermute | solution.py:22
  59.4 5.0 %copy-start.3 = (bf16[1024,256]{1,0:T(8,128)(2,1)S(1)}, bf16[1024,256]{1,0:T(8,128)(2,1)}, u32[]{:S(2)}) copy-start(bf16[1024,256]{1,0:T(8,128)(2,1)} %copy-done.2) | copy-start | bytes 1572868
  72.8 10.7 %collective-permute-start.14 = (bf16[128,1024]{1,0:T(8,128)(2,1)}, bf16[128,1024]{1,0:T(8,128)(2,1)}, u32[]{:S(2)}, u32[]{:S(2)}) collective-permute-start(bf16[128,1024]{1,0:T(8,128)(2,1)} %get-tuple-element.29), channel_id=1, source_target_pairs={{0,3},{1,0},{2,1},{3,2},{4,7},{5,4},{6,5},{7,6},{8,11},{9,8},{10,9... | collective-permute-start | bytes 786440 | tf_op jit(solution)/shard_map/ppermute | solution.py:134
  75.1 22.5 %collective-permute-start.13 = (bf16[128,1024]{1,0:T(8,128)(2,1)S(1)}, bf16[128,1024]{1,0:T(8,128)(2,1)}, u32[]{:S(2)}, u32[]{:S(2)}) collective-permute-start(bf16[128,1024]{1,0:T(8,128)(2,1)S(1)} %get-tuple-element.30), channel_id=1, source_target_pairs={{0,2},{1,3},{2,0},{3,1},{4,6},{5,7},{6,4},{7,5},{8,10},{9,11},{10,... | collective-permute-start | bytes 786440 | tf_op jit(solution)/shard_map/ppermute | solution.py:134
  75.1 22.5 %collective-permute-start.12 = (bf16[128,1024]{1,0:T(8,128)(2,1)S(1)}, bf16[128,1024]{1,0:T(8,128)(2,1)}, u32[]{:S(2)}, u32[]{:S(2)}) collective-permute-start(bf16[128,1024]{1,0:T(8,128)(2,1)S(1)} %get-tuple-element.28), channel_id=1, source_target_pairs={{0,1},{1,2},{2,3},{3,0},{4,5},{5,6},{6,7},{7,4},{8,9},{9,10},{10,1... | collective-permute-start | bytes 786440 | tf_op jit(solution)/shard_map/ppermute | solution.py:134
  75.7 40.1 %copy-start.4 = (bf16[1024,128]{1,0:T(8,128)(2,1)S(1)}, bf16[1024,128]{1,0:T(8,128)(2,1)}, u32[]{:S(2)}) copy-start(bf16[1024,128]{1,0:T(8,128)(2,1)} %param.15) | copy-start | bytes 786436
  75.7 40.1 %copy-start.5 = (f32[1024]{0:T(1024)S(1)}, f32[1024]{0:T(1024)}, u32[]{:S(2)}) copy-start(f32[1024]{0:T(1024)} %param.14) | copy-start | bytes 12292
  115.8 1.0 copy-start.6
